TPU v7x, 32 devices: a whole 2x2x4 slice. The times are simulated.
32 devices in a mesh: rot: 16 (over z, x, core), term: 2 (over y).
Axes of the slice: x: 2, y: 2, z: 4, core: 2. Of those that a mesh axis runs over, the one named last changes fastest.
Arguments:
- receptor_grids: bfloat16 [22, 128, 1024], P('term', 'rot'), may hold values from -6 to 6
- term_weights: float32 [22], P('term'), may hold values from 0.5 to 2
- atom_weights: float32 [22, 256], P('term'), may hold values from -0.125 to 0.125
- ligand_cells: int32 [3, 32, 256], P(None, 'rot'), may hold values from 0 to 15
Outputs:
- best_scores: float32 [4, 32], P(None, 'rot')
- best_overall: float32 [4], replicated
All inputs are finite; a program needn't handle non-finite values.
Results may differ from a plain program's by a relative error of at most 0.0017.
Values may be sent and summed in bfloat16 or wider, within the bound.
No kernel may reach another device: no remote copies, remote signals or barrier semaphores. Data moves between devices by JAX's collectives and lax.ppermute only.
A program may use at most 128 MiB of HBM per device.

v0:
```python
import math
import numpy as np
import jax
import jax.numpy as jnp
from jax import lax
from jax.sharding import PartitionSpec as P

G = 32
HZ = G // 2 + 1
LB = 16
HIGH = lax.Precision.HIGH
HIGHEST = lax.Precision.HIGHEST


def line_table(freq_count, cell_count):
    freq = np.arange(freq_count)[:, None]
    cell = np.arange(cell_count)[None, :]
    phase = (freq * cell % G).astype(np.float64) * (2.0 * math.pi / G)
    return (np.cos(phase).astype(np.float32), np.sin(phase).astype(np.float32))


def plane_tables(side):
    cy, sy = line_table(G, side)
    cz, sz = line_table(HZ, side)
    cy = jnp.asarray(cy.T)[:, None, :, None]
    sy = jnp.asarray(sy.T)[:, None, :, None]
    cz = jnp.asarray(cz.T)[None, :, None, :]
    sz = jnp.asarray(sz.T)[None, :, None, :]
    cos_t = (cy * cz - sy * sz).reshape(side * side, G * HZ)
    sin_t = (sy * cz + cy * sz).reshape(side * side, G * HZ)
    return (cos_t, sin_t)


def split_bf16(table):
    upper = table.astype(jnp.bfloat16)
    lower = (table - upper.astype(jnp.float32)).astype(jnp.bfloat16)
    return (upper, lower)


def mix_table(cell_count):
    cos_x, sin_x = line_table(G, cell_count)
    return jnp.asarray(np.concatenate([cos_x, sin_x], axis=0))


def dot2(rows, upper, lower):
    first = jnp.dot(rows, upper, preferred_element_type=jnp.float32)
    second = jnp.dot(rows, lower, preferred_element_type=jnp.float32)
    return first + second


def receptor_spectra(grids, cos_hi, cos_lo, sin_hi, sin_lo):
    terms, rows, cells = grids.shape
    receptors = rows // G
    flat = grids.reshape(terms * rows, cells)
    plane_re = dot2(flat, cos_hi, cos_lo).reshape(terms, receptors, G, G * HZ)
    plane_ims = dot2(flat, sin_hi, sin_lo).reshape(terms, receptors, G, G * HZ)
    mix = mix_table(G)
    mixed_re = jnp.einsum("px,trxq->trpq", mix, plane_re, precision=HIGH)
    mixed_ims = jnp.einsum("px,trxq->trpq", mix, plane_ims, precision=HIGH)
    spec_re = mixed_re[:, :, :G] - mixed_ims[:, :, G:]
    spec_im = -mixed_ims[:, :, :G] - mixed_re[:, :, G:]
    return (spec_re, spec_im)


def ligand_spectra(voxels, coefficients, box_cos, box_sin):
    rot_count = voxels.shape[1]
    terms = coefficients.shape[0]
    flat_index = (voxels[0] * LB + voxels[1]) * LB + voxels[2]
    cells = jnp.arange(LB**3, dtype=jnp.int32)
    onehot = (flat_index[:, :, None] == cells[None, None, :]).astype(jnp.float32)
    grid = jnp.einsum("ta,nac->tnc", coefficients, onehot, precision=HIGHEST)
    grid = grid.reshape(terms, rot_count, LB, LB * LB)
    plane_re = jnp.einsum("tnxc,cq->tnxq", grid, box_cos, precision=HIGH)
    plane_ims = jnp.einsum("tnxc,cq->tnxq", grid, box_sin, precision=HIGH)
    mix = mix_table(LB)
    mixed_re = jnp.einsum("px,tnxq->tnpq", mix, plane_re, precision=HIGH)
    mixed_ims = jnp.einsum("px,tnxq->tnpq", mix, plane_ims, precision=HIGH)
    lig_re = mixed_re[:, :, :G] - mixed_ims[:, :, G:]
    lig_im = -mixed_ims[:, :, :G] - mixed_re[:, :, G:]
    return (lig_re, lig_im)


def correlate(lig_re, lig_im, rec_re, rec_im):
    lr = lig_re[:, None]
    li = lig_im[:, None]
    rr = rec_re[:, :, None]
    ri = rec_im[:, :, None]
    prod_re = jnp.sum(lr * rr + li * ri, axis=0)
    prod_im = jnp.sum(lr * ri - li * rr, axis=0)
    return jnp.stack([prod_re, prod_im], axis=0)


def inverse_scores(products, cos_t, sin_t):
    mix = mix_table(G)
    mixed = jnp.einsum("xp,srnpq->srnxq", mix, products, precision=HIGH)
    inv_re = mixed[0, :, :, :G] - mixed[1, :, :, G:]
    inv_im = mixed[1, :, :, :G] + mixed[0, :, :, G:]
    freq_z = np.arange(G * HZ) % HZ
    fold = np.where((freq_z == 0) | (freq_z == G // 2), 1.0, 2.0) / float(G**3)
    fold = jnp.asarray(fold.astype(np.float32))
    scores = jnp.einsum("rnxq,cq->rnxc", inv_re * fold, cos_t, precision=HIGH)
    scores = scores - jnp.einsum("rnxq,cq->rnxc", inv_im * fold, sin_t, precision=HIGH)
    return scores


def body(receptor_grids, term_weights, atom_weights, ligand_cells):
    gathered = lax.all_gather(receptor_grids, "rot", axis=1, tiled=True)
    with jax.named_scope("twiddle_tables"):
        cos_t, sin_t = plane_tables(G)
        box_cos, box_sin = plane_tables(LB)
        cos_hi, cos_lo = split_bf16(cos_t)
        sin_hi, sin_lo = split_bf16(sin_t)
        tables = lax.optimization_barrier(
            (cos_t, sin_t, box_cos, box_sin, cos_hi, cos_lo, sin_hi, sin_lo)
        )
        cos_t, sin_t, box_cos, box_sin, cos_hi, cos_lo, sin_hi, sin_lo = tables
    with jax.named_scope("ligand_spectra"):
        coefficients = atom_weights * term_weights[:, None]
        lig_re, lig_im = ligand_spectra(ligand_cells, coefficients, box_cos, box_sin)
    with jax.named_scope("receptor_spectra"):
        rec_re, rec_im = receptor_spectra(gathered, cos_hi, cos_lo, sin_hi, sin_lo)
    with jax.named_scope("correlate"):
        products = correlate(lig_re, lig_im, rec_re, rec_im)
    products = lax.psum_scatter(products, "term", scatter_dimension=2, tiled=True)
    with jax.named_scope("inverse_scores"):
        scores = inverse_scores(products, cos_t, sin_t)
        best_here = jnp.max(scores, axis=(2, 3))
    best_all = lax.all_gather(best_here, ("rot", "term"), axis=1, tiled=True)
    rot_local = ligand_cells.shape[1]
    start = lax.axis_index("rot") * rot_local
    best_scores = lax.dynamic_slice_in_dim(best_all, start, rot_local, axis=1)
    best_overall = jnp.max(best_all, axis=1)
    return (best_scores, best_overall)


def solution(mesh):
    placed = (P("term", "rot", None), P("term"), P("term", None), P(None, "rot", None))
    return jax.shard_map(
        body, mesh=mesh, in_specs=placed, out_specs=(P(None, "rot"), P()), check_vma=False
    )
```

profile of v0, /device:TPU:0, one launch (start us, length us, event | category | flops | bytes accessed | tf_op | source)
XLA Modules:
  0.0 238.6 jit_solution(8877241703728081015)
XLA Ops:
  7.2 0.0 all-gather.3.cloned.1.call-start
  7.2 0.7 all-gather.3.cloned.1.call-update
  7.9 0.0 all-reduce.3.cloned.1.call-start
  7.9 8.2 %multiply_add_fusion = (f32[32,32,32,17]{1,0,3,2:T(8,128)}, f32[32,32,32,17]{1,0,3,2:T(8,128)}) fusion(f32[32,17]{0,1:T(8,128)} %constant.43.clone, f32[32,32]{0,1:T(8,128)} %constant.41.clone, f32[32,17]{0,1:T(8,128)} %constant.42.clone, f32[32,32]{0,1:T(8,128)} %constant.40.clone), kind=kLoop, calls=%fused_computation | loop fusion | flops 3342336 | bytes 4468992 | tf_op jit(solution)/shard_map/twiddle_tables/add | solution.py:30
  16.2 7.0 %add.65 = f32[1024,544]{0,1:T(8,128)S(1)} reshape(f32[32,32,32,17]{1,0,3,2:T(8,128)} %get-tuple-element.28) | data formatting | bytes 4456448 | tf_op jit(solution)/shard_map/twiddle_tables/add | solution.py:30
  23.2 0.0 copy-start.9
  23.2 0.0 copy-start.10
  23.2 0.0 copy-start.11
  23.2 0.0 copy-start.12
  23.2 7.9 %sub.49 = f32[1024,544]{0,1:T(8,128)} reshape(f32[32,32,32,17]{1,0,3,2:T(8,128)} %get-tuple-element.29) | data formatting | bytes 4456448 | tf_op jit(solution)/shard_map/twiddle_tables/sub | solution.py:29
  31.1 0.0 copy-done.9
  31.1 0.0 copy-done.10
  31.2 0.0 copy-done.11
  31.2 0.0 copy-done.12
  31.2 4.5 %multiply_add_fusion.1 = (f32[16,16,32,17]{3,2,1,0:T(8,128)}, f32[16,16,32,17]{3,2,1,0:T(8,128)}) fusion(f32[16,17]{1,0:T(8,128)S(1)} %copy-done.12, f32[16,32]{1,0:T(8,128)S(1)} %copy-done.10, f32[16,17]{1,0:T(8,128)S(1)} %copy-done.11, f32[16,32]{1,0:T(8,128)S(1)} %copy-done.9), kind=kLoop, calls=%fused_computation.6 | loop fusion | flops 835584 | bytes 1120384 | tf_op jit(solution)/shard_map/twiddle_tables/add | solution.py:30
  35.7 4.5 %add.67 = f32[256,544]{1,0:T(8,128)S(1)} reshape(f32[16,16,32,17]{3,2,1,0:T(8,128)} %get-tuple-element.30) | data formatting | bytes 1114112 | tf_op jit(solution)/shard_map/twiddle_tables/add | solution.py:30
  40.1 5.1 %sub.51 = f32[256,544]{1,0:T(8,128)} reshape(f32[16,16,32,17]{3,2,1,0:T(8,128)} %get-tuple-element.31) | data formatting | bytes 1114112 | tf_op jit(solution)/shard_map/twiddle_tables/sub | solution.py:29
  45.3 5.1 %subtract_convert_fusion = (bf16[1024,544]{0,1:T(8,128)(2,1)}, bf16[1024,544]{0,1:T(8,128)(2,1)}, bf16[1024,544]{0,1:T(8,128)(2,1)}, bf16[1024,544]{0,1:T(8,128)(2,1)}) fusion(f32[1024,544]{0,1:T(8,128)S(1)} %add.65, f32[1024,544]{0,1:T(8,128)} %sub.49), kind=kLoop, calls=%fused_computation.22 | loop fusion | flops 4456448 | bytes 8912896 | tf_op jit(solution)/shard_map/twiddle_tables/convert_element_type | solution.py:36
  50.4 0.0 copy-done.13
  50.4 0.0 copy-done.16
  50.4 0.0 copy-done.17
  50.4 0.0 copy-start.7
  50.4 3.6 %fusion = f32[11,2,4096]{2,0,1:T(8,128)} fusion(s32[2,256]{1,0:T(2,128)S(1)} %add_bitcast_fusion, f32[11,256]{1,0:T(8,128)S(1)} %copy-done.16, f32[11]{0:T(128)S(1)} %copy-done.17), kind=kOutput, calls=%fused_computation.3 | convolution fusion | flops 278924032 | bytes 373804 | tf_op jit(solution)/shard_map/ligand_spectra/ta,nac->tnc/dot_general | solution.py:71
  54.0 1.1 reshape.132
  55.2 0.6 fusion.15
  55.8 1.7 fusion.17
  57.5 0.0 copy-done.7
  57.5 1.6 convolution_bitcast_fusion.2
  59.1 1.6 convolution_bitcast_fusion.3
  60.7 0.0 copy-start.5
  60.7 2.3 slice_subtract_fusion.3
  63.1 0.0 copy-done.5
  63.1 3.9 %fusion.35 = f32[544,1408]{1,0:T(8,128)S(1)} fusion(bf16[1024,544]{0,1:T(8,128)(2,1)S(1)} %copy-done.5, bf16[1408,1024]{1,0:T(8,128)(2,1)} %bitcast.113), kind=kOutput, calls=%fused_computation.56 | convolution fusion | flops 1568669696 | bytes 7061504 | tf_op jit(solution)/shard_map/receptor_spectra/dot_general | solution.py:46
  67.0 0.0 copy-done.4
  67.0 0.0 copy-done.14
  67.0 3.6 %fusion.3 = f32[1408,544]{0,1:T(8,128)} fusion(f32[544,1408]{1,0:T(8,128)S(1)} %fusion.35, bf16[1024,544]{0,1:T(8,128)(2,1)S(1)} %copy-done.4, bf16[1408,1024]{1,0:T(8,128)(2,1)S(1)} %bitcast.115), kind=kOutput, calls=%fused_computation.15 | convolution fusion | flops 1569435648 | bytes 10125312 | tf_op jit(solution)/shard_map/receptor_spectra/dot_general | solution.py:47
  70.6 4.9 %copy.44 = f32[1408,544]{1,0:T(8,128)} copy(f32[1408,544]{0,1:T(8,128)} %fusion.3) | data formatting | bytes 6127616 | tf_op jit(solution)/shard_map/receptor_spectra/add | solution.py:48
  75.5 0.0 copy-done.3
  75.5 3.9 %fusion.36 = f32[544,1408]{1,0:T(8,128)S(1)} fusion(bf16[1024,544]{0,1:T(8,128)(2,1)S(1)} %copy-done.3, bf16[1408,1024]{1,0:T(8,128)(2,1)} %bitcast.114), kind=kOutput, calls=%fused_computation.57 | convolution fusion | flops 1568669696 | bytes 7061504 | tf_op jit(solution)/shard_map/receptor_spectra/dot_general | solution.py:46
  79.4 0.0 copy-done.2
  79.4 0.0 copy-done.15
  79.4 3.6 %fusion.2 = f32[1408,544]{0,1:T(8,128)} fusion(f32[544,1408]{1,0:T(8,128)S(1)} %fusion.36, bf16[1024,544]{0,1:T(8,128)(2,1)S(1)} %copy-done.2, bf16[1408,1024]{1,0:T(8,128)(2,1)S(1)} %bitcast.116), kind=kOutput, calls=%fused_computation.13 | convolution fusion | flops 1569435648 | bytes 10125312 | tf_op jit(solution)/shard_map/receptor_spectra/dot_general | solution.py:47
  83.0 4.8 %copy.45 = f32[1408,544]{1,0:T(8,128)} copy(f32[1408,544]{0,1:T(8,128)} %fusion.2) | data formatting | bytes 6127616 | tf_op jit(solution)/shard_map/receptor_spectra/add | solution.py:48
  87.9 0.0 copy-done.6
  87.9 5.2 %convolution_bitcast_fusion.1 = f32[11,4,64,544]{3,2,1,0:T(8,128)S(1)} fusion(f32[11,4,32,544]{3,2,1,0:T(8,128)} %bitcast.105, f32[64,32,1,1]{0,1,3,2:T(8,128)S(1)} %copy-done.6), kind=kOutput, calls=%fused_computation.17 | convolution fusion | flops 294125568 | bytes 9199616 | tf_op jit(solution)/shard_map/receptor_spectra/px,trxq->trpq/dot_general | solution.py:58
  93.1 0.0 copy-done.1
  93.1 5.1 %convolution_bitcast_fusion = f32[11,4,64,544]{3,2,1,0:T(8,128)} fusion(f32[11,4,32,544]{3,2,1,0:T(8,128)S(1)} %bitcast.106, f32[64,32,1,1]{0,1,3,2:T(8,128)S(1)} %copy-done.6), kind=kOutput, calls=%fused_computation.16 | convolution fusion | flops 294125568 | bytes 9199616 | tf_op jit(solution)/shard_map/receptor_spectra/px,trxq->trpq/dot_general | solution.py:59
  98.2 6.6 %slice_subtract_fusion.1 = (f32[11,4,32,544]{3,2,1,0:T(8,128)S(1)}, f32[11,4,32,544]{3,2,1,0:T(8,128)}) fusion(f32[11,4,64,544]{3,2,1,0:T(8,128)} %convolution_bitcast_fusion, f32[11,4,64,544]{3,2,1,0:T(8,128)S(1)} %convolution_bitcast_fusion.1), kind=kLoop, calls=%fused_computation.11 | loop fusion | flops 2297856 | bytes 18382848 | tf_op jit(solution)/shard_map/receptor_spectra/sub | solution.py:60
  104.8 4.6 %add_reduce_fusion = (f32[4,2,32,544]{3,2,1,0:T(8,128)S(1)}, f32[4,2,32,544]{3,2,1,0:T(8,128)S(1)}) fusion(f32[11,4,32,544]{3,2,1,0:T(8,128)} %get-tuple-element.25, f32[11,2,32,544]{3,2,1,0:T(8,128)} %get-tuple-element.27, f32[11,4,32,544]{3,2,1,0:T(8,128)S(1)} %get-tuple-element.24, f32[11,2,32,544]{3,2,1,0:T(8,128)} %get-tuple-element.26), kind=kLoop, calls=%fused_computation.5 | loop fusion | flops 11976704 | bytes 10305536 | tf_op jit(solution)/shard_map/correlate/reduce_sum | solution.py:88
  109.5 0.0 copy-start.18
  109.5 0.0 copy-start.8
  109.5 1.2 pad_maximum_fusion
  110.7 0.0 all-reduce.3.cloned.1.call-update
  110.7 0.0 copy-done.18
  110.7 0.6 dynamic-slice.2
  111.3 48.1 %all-reduce.3.cloned.1.call-done = f32[2,4,2,32,544]{4,3,2,1,0:T(8,128)} async-done(((f32[2,4,2,32,544]{4,3,2,1,0:T(8,128)}), f32[2,4,2,32,544]{4,3,2,1,0:T(8,128)}) %all-reduce.3.cloned.1.call-update) | async-done | bytes 1114128
  159.4 2.6 %fusion.14 = f32[2,4,544,64]{2,3,1,0:T(8,128)S(1)} fusion(f32[64,32,1,1]{0,1,3,2:T(8,128)S(1)} %copy-done.6, f32[2,4,2,32,544]{4,3,2,1,0:T(8,128)} %all-reduce.3.cloned.1.call-done, u32[]{:T(128)} %bitcast.40), kind=kOutput, calls=%fused_computation.33 | convolution fusion | flops 53477376 | bytes 1778176 | tf_op jit(solution)/shard_map/inverse_scores/xp,srnpq->srnxq/dot_general | solution.py:95
  162.0 0.0 copy-done.8
  162.0 0.9 fusion.4
  163.0 0.0 copy-done
  163.0 1.1 fusion.11
  164.1 66.6 %all-gather = f32[32,1,4]{2,1,0:T(1,128)S(1)} all-gather(f32[1,1,4]{2,1,0:T(1,128)S(1)} %bitcast.111), channel_id=1, replica_groups=mesh['rot'=16,'term'=2] {'rot','term'}, dimensions={0}, use_global_device_ids=true | all-gather | bytes 528 | tf_op jit(solution)/shard_map/all_gather | solution.py:128
  230.7 0.6 constant_dynamic-slice_fusion
  231.2 0.6 reduce_max.22
  (13 shorter events, 0.0 us)
Async XLA Ops:
  7.2 55.9 %all-gather.3.cloned.1.call-start = ((), (), s32[]{:S(2)}) async-start(), calls=%async_computation | async-start | bytes 3063808 | tf_op jit(solution)/shard_map/all_gather | solution.py:107
  7.9 151.5 %all-reduce.3.cloned.1.call-start = ((), (), s32[]{:S(2)}) async-start(), calls=%async_computation.1 | async-start | bytes 2621440
  23.2 8.0 %copy-start.9 = (f32[16,32]{1,0:T(8,128)S(1)}, f32[16,32]{1,0:T(8,128)}, u32[]{:S(2)}) copy-start(f32[16,32]{1,0:T(8,128)} %constant.44.clone) | copy-start | bytes 6148
  23.2 8.0 %copy-start.10 = (f32[16,32]{1,0:T(8,128)S(1)}, f32[16,32]{1,0:T(8,128)}, u32[]{:S(2)}) copy-start(f32[16,32]{1,0:T(8,128)} %constant.45.clone) | copy-start | bytes 6148
  23.2 7.9 %copy-start.11 = (f32[16,17]{1,0:T(8,128)S(1)}, f32[16,17]{1,0:T(8,128)}, u32[]{:S(2)}) copy-start(f32[16,17]{1,0:T(8,128)} %constant.46.clone) | copy-start | bytes 3268
  23.2 7.9 %copy-start.12 = (f32[16,17]{1,0:T(8,128)S(1)}, f32[16,17]{1,0:T(8,128)}, u32[]{:S(2)}) copy-start(f32[16,17]{1,0:T(8,128)} %constant.47.clone) | copy-start | bytes 3268
  45.3 5.1 %copy-start.13 = (s32[3,2,256]{2,1,0:T(2,128)S(1)}, s32[3,2,256]{2,1,0:T(2,128)}, u32[]{:S(2)}) copy-start(s32[3,2,256]{2,1,0:T(2,128)} %param.19) | copy-start | bytes 18436
  45.3 5.1 %copy-start.16 = (f32[11,256]{1,0:T(8,128)S(1)}, f32[11,256]{1,0:T(8,128)}, u32[]{:S(2)}) copy-start(f32[11,256]{1,0:T(8,128)} %param.18) | copy-start | bytes 33796
  45.3 5.2 %copy-start.17 = (f32[11]{0:T(128)S(1)}, f32[11]{0:T(128)}, u32[]{:S(2)}) copy-start(f32[11]{0:T(128)} %param.17) | copy-start | bytes 136
  50.4 7.1 %copy-start.7 = (f32[64,16,1,1]{0,1,3,2:T(8,128)S(1)}, f32[64,16,1,1]{0,1,3,2:T(8,128)}, u32[]{:S(2)}) copy-start(f32[64,16,1,1]{0,1,3,2:T(8,128)} %constant.60) | copy-start | bytes 12292
  60.7 2.3 copy-start.5
  63.1 3.9 %copy-start.4 = (bf16[1024,544]{0,1:T(8,128)(2,1)S(1)}, bf16[1024,544]{0,1:T(8,128)(2,1)}, u32[]{:S(2)}) copy-start(bf16[1024,544]{0,1:T(8,128)(2,1)} %get-tuple-element.13) | copy-start | bytes 3342340
  63.1 3.9 %copy-start.14 = (bf16[11,128,1024]{2,1,0:T(8,128)(2,1)S(1)}, bf16[11,128,1024]{2,1,0:T(8,128)(2,1)}, u32[]{:S(2)}) copy-start(bf16[11,128,1024]{2,1,0:T(8,128)(2,1)} %all-gather.3.cloned.1.call-done) | copy-start | bytes 8650756
  70.6 4.9 %copy-start.3 = (bf16[1024,544]{0,1:T(8,128)(2,1)S(1)}, bf16[1024,544]{0,1:T(8,128)(2,1)}, u32[]{:S(2)}) copy-start(bf16[1024,544]{0,1:T(8,128)(2,1)} %get-tuple-element.14) | copy-start | bytes 3342340
  75.5 3.9 %copy-start.2 = (bf16[1024,544]{0,1:T(8,128)(2,1)S(1)}, bf16[1024,544]{0,1:T(8,128)(2,1)}, u32[]{:S(2)}) copy-start(bf16[1024,544]{0,1:T(8,128)(2,1)} %get-tuple-element.15) | copy-start | bytes 3342340
  75.5 3.9 %copy-start.15 = (bf16[11,128,1024]{2,1,0:T(8,128)(2,1)S(1)}, bf16[11,128,1024]{2,1,0:T(8,128)(2,1)}, u32[]{:S(2)}) copy-start(bf16[11,128,1024]{2,1,0:T(8,128)(2,1)} %all-gather.3.cloned.1.call-done) | copy-start | bytes 8650756
  83.0 4.8 %copy-start.6 = (f32[64,32,1,1]{0,1,3,2:T(8,128)S(1)}, f32[64,32,1,1]{0,1,3,2:T(8,128)}, u32[]{:S(2)}) copy-start(f32[64,32,1,1]{0,1,3,2:T(8,128)} %constant.61) | copy-start | bytes 24580
  87.9 5.2 %copy-start.1 = (f32[1408,544]{1,0:T(8,128)S(1)}, f32[1408,544]{1,0:T(8,128)}, u32[]{:S(2)}) copy-start(f32[1408,544]{1,0:T(8,128)} %copy.45) | copy-start | bytes 9191428
  109.5 1.3 copy-start.18
  109.5 52.6 %copy-start.8 = (f32[544]{0:T(1024)S(1)}, f32[544]{0:T(1024)}, u32[]{:S(2)}) copy-start(f32[544]{0:T(1024)} %constant.50.clone) | copy-start | bytes 6532
  159.4 3.6 %copy-start = (f32[1024,544]{0,1:T(8,128)S(1)}, f32[1024,544]{0,1:T(8,128)}, u32[]{:S(2)}) copy-start(f32[1024,544]{0,1:T(8,128)} %sub.49) | copy-start | bytes 6684676
Sparse Core Ops, SparseCore 0:
  10.2 47.0 all-gather.2
  110.8 48.5 all-reduce.2
where the time goes:
time: 239 us
  blocking collectives  66.6 us (28%)
  waiting for transfers between devices  48.8 us (20%)
  matrix products  39.1 us (16%)
  local copies, waits for them, and re-layouts  36.6 us (15%)
  other arithmetic  33.2 us (14%)
  between operations  14.3 us (6%)
    all_gather x1, blocking collectives, body(): best_all = lax.all_gather(best_here, ('rot', 'term'), axis=1, tiled=True)  66.6 us
    unnamed x3, waiting for transfers between devices  48.8 us
    sub x2, local copies, waits for them, and re-layouts, plane_tables(): cos_t = (cy * cz - sy * sz).reshape(side * side, G * HZ)  13 us
    add x2, other arithmetic, plane_tables(): sin_t = (sy * cz + cy * sz).reshape(side * side, G * HZ)  12.7 us
    add x2, local copies, waits for them, and re-layouts, plane_tables(): sin_t = (sy * cz + cy * sz).reshape(side * side, G * HZ)  11.5 us
    add x2, local copies, waits for them, and re-layouts, dot2(): return first + second  9.7 us
    dot_general x2, matrix products, dot2(): first = jnp.dot(rows, upper, preferred_element_type=jnp.float32)  7.78 us
    dot_general x2, matrix products, dot2(): second = jnp.dot(rows, lower, preferred_element_type=jnp.float32)  7.23 us
  transfers between devices with their start and end apart: 2, of which 1 were waited for; matrix products, arithmetic and copies ran while one was open for 23% of the time, Pallas kernels for 0%

commit v1 on v0

--- a/solution.py
+++ b/solution.py
@@ -10,6 +10,23 @@
 LB = 16
 HIGH = lax.Precision.HIGH
 HIGHEST = lax.Precision.HIGHEST
+
+
+def joined_along(blocks, dim):
+    lengths = list(blocks.shape[1:])
+    lengths[dim] *= blocks.shape[0]
+    return jnp.moveaxis(blocks, 0, dim).reshape(lengths)
+
+
+def collected_by_bits(x, axis):
+    peers, index = (lax.axis_size(axis), lax.axis_index(axis))
+    parts, distance = (x[None], 1)
+    while distance < peers:
+        other = lax.ppermute(parts, axis, [(i, i ^ distance) for i in range(peers)])
+        low = index & distance == 0
+        parts = jnp.concatenate([jnp.where(low, parts, other), jnp.where(low, other, parts)])
+        distance *= 2
+    return parts
 
 
 def line_table(freq_count, cell_count):
@@ -125,7 +142,7 @@
     with jax.named_scope("inverse_scores"):
         scores = inverse_scores(products, cos_t, sin_t)
         best_here = jnp.max(scores, axis=(2, 3))
-    best_all = lax.all_gather(best_here, ("rot", "term"), axis=1, tiled=True)
+    best_all = joined_along(collected_by_bits(best_here, ("rot", "term")), 1)
     rot_local = ligand_cells.shape[1]
     start = lax.axis_index("rot") * rot_local
     best_scores = lax.dynamic_slice_in_dim(best_all, start, rot_local, axis=1)

time: 239 us -> 191 us (0.80)
  blocking collectives: 66.6 us -> 0 us
  waiting for transfers between devices: 48.8 us -> 59.5 us
  starting transfers between devices: 0.08 us -> 6 us
    all_gather x1 -> x0, blocking collectives: 66.6 us -> none  [body(): best_all = lax.all_gather(best_here, ('rot', 'term'), axis=1, tiled=True)]
    ppermute x0 -> x5, waiting for transfers between devices: none -> 10.7 us  [collected_by_bits(): other = lax.ppermute(parts, axis, [(i, i ^ distance) for i in range(peers)])]
    ppermute x0 -> x5, starting transfers between devices: none -> 5.93 us  [collected_by_bits(): other = lax.ppermute(parts, axis, [(i, i ^ distance) for i in range(peers)])]
  transfers between devices with their start and end apart: 2 -> 7, of which waited for: 1 -> 6; matrix products, arithmetic and copies ran while one was open for 23% -> 29% of each run, Pallas kernels for 0% -> 0%
where the time goes in v1:
time: 191 us
  waiting for transfers between devices  59.5 us (31%)
  matrix products  38.9 us (20%)
  local copies, waits for them, and re-layouts  36.9 us (19%)
  other arithmetic  35.3 us (18%)
  between operations  14.4 us (8%)
  starting transfers between devices  6 us (3%)
    unnamed x3, waiting for transfers between devices  48.8 us
    sub x2, local copies, waits for them, and re-layouts, plane_tables(): cos_t = (cy * cz - sy * sz).reshape(side * side, G * HZ)  13.1 us
    add x2, other arithmetic, plane_tables(): sin_t = (sy * cz + cy * sz).reshape(side * side, G * HZ)  12.8 us
    add x2, local copies, waits for them, and re-layouts, plane_tables(): sin_t = (sy * cz + cy * sz).reshape(side * side, G * HZ)  11.5 us
    ppermute x5, waiting for transfers between devices, collected_by_bits(): other = lax.ppermute(parts, axis, [(i, i ^ distance) for i in range(peers)])  10.7 us
    add x2, local copies, waits for them, and re-layouts, dot2(): return first + second  9.67 us
    dot_general x2, matrix products, dot2(): first = jnp.dot(rows, upper, preferred_element_type=jnp.float32)  7.78 us
    sub x1, other arithmetic, receptor_spectra(): spec_re = mixed_re[:, :, :G] - mixed_ims[:, :, G:]  7.76 us
  transfers between devices with their start and end apart: 7, of which 6 were waited for; matrix products, arithmetic and copies ran while one was open for 29% of the time, Pallas kernels for 0%

profile of v1, /device:TPU:0, one launch (start us, length us, event | category | flops | bytes accessed | tf_op | source)
XLA Modules:
  0.0 190.9 jit_solution(16604146344426126184)
XLA Ops:
  7.2 0.0 all-gather.2.cloned.1.call-start
  7.2 0.7 all-gather.2.cloned.1.call-update
  7.9 0.0 all-reduce.3.cloned.1.call-start
  7.9 8.3 %multiply_add_fusion = (f32[32,32,32,17]{1,0,3,2:T(8,128)}, f32[32,32,32,17]{1,0,3,2:T(8,128)}) fusion(f32[32,17]{0,1:T(8,128)} %constant.53.clone, f32[32,32]{0,1:T(8,128)} %constant.51.clone, f32[32,17]{0,1:T(8,128)} %constant.52.clone, f32[32,32]{0,1:T(8,128)} %constant.50.clone), kind=kLoop, calls=%fused_computation | loop fusion | flops 3342336 | bytes 4468992 | tf_op jit(solution)/shard_map/twiddle_tables/add | solution.py:47
  16.2 7.0 %add.69 = f32[1024,544]{0,1:T(8,128)S(1)} reshape(f32[32,32,32,17]{1,0,3,2:T(8,128)} %get-tuple-element.32) | data formatting | bytes 4456448 | tf_op jit(solution)/shard_map/twiddle_tables/add | solution.py:47
  23.3 0.0 copy-start.10
  23.3 0.0 copy-start.11
  23.3 0.0 copy-start.12
  23.3 0.0 copy-start.13
  23.3 7.9 %sub.49 = f32[1024,544]{0,1:T(8,128)} reshape(f32[32,32,32,17]{1,0,3,2:T(8,128)} %get-tuple-element.33) | data formatting | bytes 4456448 | tf_op jit(solution)/shard_map/twiddle_tables/sub | solution.py:46
  31.2 0.0 copy-done.12
  31.2 0.0 copy-done.13
  31.3 4.5 %multiply_add_fusion.1 = (f32[16,16,32,17]{3,2,1,0:T(8,128)}, f32[16,16,32,17]{3,2,1,0:T(8,128)}) fusion(f32[16,17]{1,0:T(8,128)S(1)} %copy-done.13, f32[16,32]{1,0:T(8,128)S(1)} %copy-done.11, f32[16,17]{1,0:T(8,128)S(1)} %copy-done.12, f32[16,32]{1,0:T(8,128)S(1)} %copy-done.10), kind=kLoop, calls=%fused_computation.6 | loop fusion | flops 835584 | bytes 1120384 | tf_op jit(solution)/shard_map/twiddle_tables/add | solution.py:47
  35.8 4.5 %add.71 = f32[256,544]{1,0:T(8,128)S(1)} reshape(f32[16,16,32,17]{3,2,1,0:T(8,128)} %get-tuple-element.34) | data formatting | bytes 1114112 | tf_op jit(solution)/shard_map/twiddle_tables/add | solution.py:47
  40.3 5.1 %sub.51 = f32[256,544]{1,0:T(8,128)} reshape(f32[16,16,32,17]{3,2,1,0:T(8,128)} %get-tuple-element.35) | data formatting | bytes 1114112 | tf_op jit(solution)/shard_map/twiddle_tables/sub | solution.py:46
  45.4 5.1 %subtract_convert_fusion = (bf16[1024,544]{0,1:T(8,128)(2,1)}, bf16[1024,544]{0,1:T(8,128)(2,1)}, bf16[1024,544]{0,1:T(8,128)(2,1)}, bf16[1024,544]{0,1:T(8,128)(2,1)}) fusion(f32[1024,544]{0,1:T(8,128)S(1)} %add.69, f32[1024,544]{0,1:T(8,128)} %sub.49), kind=kLoop, calls=%fused_computation.22 | loop fusion | flops 4456448 | bytes 8912896 | tf_op jit(solution)/shard_map/twiddle_tables/convert_element_type | solution.py:53
  50.5 0.0 copy-done.14
  50.5 0.0 copy-done.17
  50.5 0.0 copy-done.18
  50.5 0.0 copy-start.8
  50.5 3.6 %fusion = f32[11,2,4096]{2,0,1:T(8,128)} fusion(s32[2,256]{1,0:T(2,128)S(1)} %add_bitcast_fusion, f32[11,256]{1,0:T(8,128)S(1)} %copy-done.17, f32[11]{0:T(128)S(1)} %copy-done.18), kind=kOutput, calls=%fused_computation.3 | convolution fusion | flops 278924032 | bytes 373804 | tf_op jit(solution)/shard_map/ligand_spectra/ta,nac->tnc/dot_general | solution.py:88
  54.1 1.1 reshape.129
  55.3 0.6 fusion.15
  55.9 1.7 fusion.17
  57.6 1.6 convolution_bitcast_fusion.2
  59.2 1.6 convolution_bitcast_fusion.3
  60.9 2.4 %slice_subtract_fusion.3 = (f32[11,2,32,544]{3,2,1,0:T(8,128)}, f32[11,2,32,544]{3,2,1,0:T(8,128)}) fusion(f32[11,2,64,544]{3,2,1,0:T(8,128)S(1)} %convolution_bitcast_fusion.2, f32[11,2,64,544]{3,2,1,0:T(8,128)S(1)} %convolution_bitcast_fusion.3), kind=kLoop, calls=%fused_computation.28 | loop fusion | flops 1148928 | bytes 9191424 | tf_op jit(solution)/shard_map/ligand_spectra/sub | solution.py:95
  63.3 3.9 %fusion.37 = f32[544,1408]{1,0:T(8,128)S(1)} fusion(bf16[1024,544]{0,1:T(8,128)(2,1)S(1)} %copy-done.6, bf16[1408,1024]{1,0:T(8,128)(2,1)} %bitcast.115), kind=kOutput, calls=%fused_computation.73 | convolution fusion | flops 1568669696 | bytes 7061504 | tf_op jit(solution)/shard_map/receptor_spectra/dot_general | solution.py:63
  67.2 3.5 %fusion.3 = f32[1408,544]{0,1:T(8,128)} fusion(f32[544,1408]{1,0:T(8,128)S(1)} %fusion.37, bf16[1024,544]{0,1:T(8,128)(2,1)S(1)} %copy-done.5, bf16[1408,1024]{1,0:T(8,128)(2,1)S(1)} %bitcast.117), kind=kOutput, calls=%fused_computation.15 | convolution fusion | flops 1569435648 | bytes 10125312 | tf_op jit(solution)/shard_map/receptor_spectra/dot_general | solution.py:64
  70.7 4.9 %copy.50 = f32[1408,544]{1,0:T(8,128)} copy(f32[1408,544]{0,1:T(8,128)} %fusion.3) | data formatting | bytes 6127616 | tf_op jit(solution)/shard_map/receptor_spectra/add | solution.py:65
  75.6 3.9 %fusion.38 = f32[544,1408]{1,0:T(8,128)S(1)} fusion(bf16[1024,544]{0,1:T(8,128)(2,1)S(1)} %copy-done.4, bf16[1408,1024]{1,0:T(8,128)(2,1)} %bitcast.116), kind=kOutput, calls=%fused_computation.74 | convolution fusion | flops 1568669696 | bytes 7061504 | tf_op jit(solution)/shard_map/receptor_spectra/dot_general | solution.py:63
  79.5 3.5 %fusion.2 = f32[1408,544]{0,1:T(8,128)} fusion(f32[544,1408]{1,0:T(8,128)S(1)} %fusion.38, bf16[1024,544]{0,1:T(8,128)(2,1)S(1)} %copy-done.3, bf16[1408,1024]{1,0:T(8,128)(2,1)S(1)} %bitcast.118), kind=kOutput, calls=%fused_computation.13 | convolution fusion | flops 1569435648 | bytes 10125312 | tf_op jit(solution)/shard_map/receptor_spectra/dot_general | solution.py:64
  83.1 4.8 %copy.51 = f32[1408,544]{1,0:T(8,128)} copy(f32[1408,544]{0,1:T(8,128)} %fusion.2) | data formatting | bytes 6127616 | tf_op jit(solution)/shard_map/receptor_spectra/add | solution.py:65
  87.9 5.2 %convolution_bitcast_fusion.1 = f32[11,4,64,544]{3,2,1,0:T(8,128)S(1)} fusion(f32[11,4,32,544]{3,2,1,0:T(8,128)} %bitcast.107, f32[64,32,1,1]{0,1,3,2:T(8,128)S(1)} %copy-done.7), kind=kOutput, calls=%fused_computation.17 | convolution fusion | flops 294125568 | bytes 9199616 | tf_op jit(solution)/shard_map/receptor_spectra/px,trxq->trpq/dot_general | solution.py:75
  93.1 5.0 %convolution_bitcast_fusion = f32[11,4,64,544]{3,2,1,0:T(8,128)} fusion(f32[11,4,32,544]{3,2,1,0:T(8,128)S(1)} %bitcast.108, f32[64,32,1,1]{0,1,3,2:T(8,128)S(1)} %copy-done.7), kind=kOutput, calls=%fused_computation.16 | convolution fusion | flops 294125568 | bytes 9199616 | tf_op jit(solution)/shard_map/receptor_spectra/px,trxq->trpq/dot_general | solution.py:76
  98.1 7.8 %slice_subtract_fusion.1 = (f32[11,4,32,544]{3,2,1,0:T(8,128)}, f32[11,4,32,544]{3,2,1,0:T(8,128)}) fusion(f32[11,4,64,544]{3,2,1,0:T(8,128)} %convolution_bitcast_fusion, f32[11,4,64,544]{3,2,1,0:T(8,128)S(1)} %convolution_bitcast_fusion.1), kind=kLoop, calls=%fused_computation.11 | loop fusion | flops 2297856 | bytes 18382848 | tf_op jit(solution)/shard_map/receptor_spectra/sub | solution.py:77
  105.9 5.1 %add_reduce_fusion = (f32[4,2,32,544]{3,2,1,0:T(8,128)S(1)}, f32[4,2,32,544]{3,2,1,0:T(8,128)S(1)}) fusion(f32[11,4,32,544]{3,2,1,0:T(8,128)} %get-tuple-element.29, f32[11,2,32,544]{3,2,1,0:T(8,128)} %get-tuple-element.31, f32[11,4,32,544]{3,2,1,0:T(8,128)} %get-tuple-element.28, f32[11,2,32,544]{3,2,1,0:T(8,128)S(1)} %copy-done.2), kind=kLoop, calls=%fused_computation.5 | loop fusion | flops 11976704 | bytes 10305536 | tf_op jit(solution)/shard_map/correlate/reduce_sum | solution.py:105
  111.1 0.0 copy-start.19
  111.1 0.0 copy-start.9
  111.1 1.2 pad_maximum_fusion
  112.3 0.0 all-reduce.3.cloned.1.call-update
  112.3 0.6 dynamic-slice.5
  112.9 48.1 %all-reduce.3.cloned.1.call-done = f32[2,4,2,32,544]{4,3,2,1,0:T(8,128)} async-done(((f32[2,4,2,32,544]{4,3,2,1,0:T(8,128)}), f32[2,4,2,32,544]{4,3,2,1,0:T(8,128)}) %all-reduce.3.cloned.1.call-update) | async-done | bytes 1114128
  161.0 2.6 %fusion.14 = f32[2,4,544,64]{2,3,1,0:T(8,128)S(1)} fusion(f32[64,32,1,1]{0,1,3,2:T(8,128)S(1)} %copy-done.7, f32[2,4,2,32,544]{4,3,2,1,0:T(8,128)} %all-reduce.3.cloned.1.call-done, u32[]{:T(128)} %bitcast.40), kind=kOutput, calls=%fused_computation.33 | convolution fusion | flops 53477376 | bytes 1778176 | tf_op jit(solution)/shard_map/inverse_scores/xp,srnpq->srnxq/dot_general | solution.py:112
  163.6 0.9 fusion.4
  164.6 1.1 fusion.11
  165.7 0.4 collective-permute-start
  166.1 3.2 %collective-permute-done = f32[1,4,1]{1,2,0:T(1,128)S(1)} collective-permute-done((f32[1,4,1]{1,2,0:T(1,128)S(1)}, f32[1,4,1]{1,2,0:T(1,128)S(1)}, u32[]{:S(2)}, u32[]{:S(2)}) %collective-permute-start) | collective-permute-done | bytes 48 | tf_op jit(solution)/shard_map/ppermute | solution.py:25
  169.3 0.1 collective-permute-start.1
  169.4 1.1 collective-permute-done.1
  170.5 1.5 collective-permute-start.2
  172.1 2.1 %collective-permute-done.2 = f32[4,4,1]{1,2,0:T(1,128)S(1)} collective-permute-done((f32[4,4,1]{1,2,0:T(1,128)S(1)}, f32[4,4,1]{1,2,0:T(1,128)S(1)}, u32[]{:S(2)}, u32[]{:S(2)}) %collective-permute-start.2) | collective-permute-done | bytes 96 | tf_op jit(solution)/shard_map/ppermute | solution.py:25
  174.2 1.5 collective-permute-start.3
  175.8 2.1 %collective-permute-done.3 = f32[8,4,1]{1,2,0:T(1,128)S(1)} collective-permute-done((f32[8,4,1]{1,2,0:T(1,128)S(1)}, f32[8,4,1]{1,2,0:T(1,128)S(1)}, u32[]{:S(2)}, u32[]{:S(2)}) %collective-permute-start.3) | collective-permute-done | bytes 160 | tf_op jit(solution)/shard_map/ppermute | solution.py:25
  177.9 0.1 copy.54
  178.0 0.1 copy.55
  178.1 0.1 pad_maximum_fusion.3
  178.1 2.4 %collective-permute-start.4 = (f32[16,4,1]{0,1,2:T(4,128)S(1)}, f32[16,4,1]{0,1,2:T(4,128)S(1)}, u32[]{:S(2)}, u32[]{:S(2)}) collective-permute-start(f32[16,4,1]{0,1,2:T(4,128)S(1)} %pad_maximum_fusion.3), channel_id=1, source_target_pairs={{0,16},{1,17},{2,18},{3,19},{4,20},{5,21},{6,22},{7,23},{8,24},{9,... | collective-permute-start | bytes 776 | tf_op jit(solution)/shard_map/ppermute | solution.py:25
  180.5 2.1 %collective-permute-done.4 = f32[16,4,1]{0,1,2:T(4,128)S(1)} collective-permute-done((f32[16,4,1]{0,1,2:T(4,128)S(1)}, f32[16,4,1]{0,1,2:T(4,128)S(1)}, u32[]{:S(2)}, u32[]{:S(2)}) %collective-permute-start.4) | collective-permute-done | bytes 288 | tf_op jit(solution)/shard_map/ppermute | solution.py:25
  182.6 0.1 fusion.36
  182.8 0.1 pad_maximum_fusion.4
  182.8 0.1 dynamic-slice_bitcast_fusion.2
  182.9 0.7 copy.56
  183.6 0.5 reduce_max.29
  (37 shorter events, 0.1 us)
Async XLA Ops:
  7.2 56.1 %all-gather.2.cloned.1.call-start = ((), (), s32[]{:S(2)}) async-start(), calls=%async_computation | async-start | bytes 3063808 | tf_op jit(solution)/shard_map/all_gather | solution.py:124
  7.9 153.1 %all-reduce.3.cloned.1.call-start = ((), (), s32[]{:S(2)}) async-start(), calls=%async_computation.1 | async-start | bytes 2621440
  23.3 8.0 %copy-start.10 = (f32[16,32]{1,0:T(8,128)S(1)}, f32[16,32]{1,0:T(8,128)}, u32[]{:S(2)}) copy-start(f32[16,32]{1,0:T(8,128)} %constant.54.clone) | copy-start | bytes 6148
  23.3 8.0 %copy-start.11 = (f32[16,32]{1,0:T(8,128)S(1)}, f32[16,32]{1,0:T(8,128)}, u32[]{:S(2)}) copy-start(f32[16,32]{1,0:T(8,128)} %constant.55.clone) | copy-start | bytes 6148
  23.3 8.0 %copy-start.12 = (f32[16,17]{1,0:T(8,128)S(1)}, f32[16,17]{1,0:T(8,128)}, u32[]{:S(2)}) copy-start(f32[16,17]{1,0:T(8,128)} %constant.56.clone) | copy-start | bytes 3268
  23.3 8.0 %copy-start.13 = (f32[16,17]{1,0:T(8,128)S(1)}, f32[16,17]{1,0:T(8,128)}, u32[]{:S(2)}) copy-start(f32[16,17]{1,0:T(8,128)} %constant.57.clone) | copy-start | bytes 3268
  45.4 5.1 %copy-start.14 = (s32[3,2,256]{2,1,0:T(2,128)S(1)}, s32[3,2,256]{2,1,0:T(2,128)}, u32[]{:S(2)}) copy-start(s32[3,2,256]{2,1,0:T(2,128)} %param.19) | copy-start | bytes 18436
  45.4 5.1 %copy-start.17 = (f32[11,256]{1,0:T(8,128)S(1)}, f32[11,256]{1,0:T(8,128)}, u32[]{:S(2)}) copy-start(f32[11,256]{1,0:T(8,128)} %param.18) | copy-start | bytes 33796
  45.4 5.1 %copy-start.18 = (f32[11]{0:T(128)S(1)}, f32[11]{0:T(128)}, u32[]{:S(2)}) copy-start(f32[11]{0:T(128)} %param.17) | copy-start | bytes 136
  50.5 7.1 %copy-start.8 = (f32[64,16,1,1]{0,1,3,2:T(8,128)S(1)}, f32[64,16,1,1]{0,1,3,2:T(8,128)}, u32[]{:S(2)}) copy-start(f32[64,16,1,1]{0,1,3,2:T(8,128)} %constant.69) | copy-start | bytes 12292
  60.8 2.4 %copy-start.6 = (bf16[1024,544]{0,1:T(8,128)(2,1)S(1)}, bf16[1024,544]{0,1:T(8,128)(2,1)}, u32[]{:S(2)}) copy-start(bf16[1024,544]{0,1:T(8,128)(2,1)} %get-tuple-element.12) | copy-start | bytes 3342340
  63.3 3.9 %copy-start.5 = (bf16[1024,544]{0,1:T(8,128)(2,1)S(1)}, bf16[1024,544]{0,1:T(8,128)(2,1)}, u32[]{:S(2)}) copy-start(bf16[1024,544]{0,1:T(8,128)(2,1)} %get-tuple-element.13) | copy-start | bytes 3342340
  63.3 3.9 %copy-start.15 = (bf16[11,128,1024]{2,1,0:T(8,128)(2,1)S(1)}, bf16[11,128,1024]{2,1,0:T(8,128)(2,1)}, u32[]{:S(2)}) copy-start(bf16[11,128,1024]{2,1,0:T(8,128)(2,1)} %all-gather.2.cloned.1.call-done) | copy-start | bytes 8650756
  70.7 4.9 %copy-start.4 = (bf16[1024,544]{0,1:T(8,128)(2,1)S(1)}, bf16[1024,544]{0,1:T(8,128)(2,1)}, u32[]{:S(2)}) copy-start(bf16[1024,544]{0,1:T(8,128)(2,1)} %get-tuple-element.14) | copy-start | bytes 3342340
  75.6 3.9 %copy-start.3 = (bf16[1024,544]{0,1:T(8,128)(2,1)S(1)}, bf16[1024,544]{0,1:T(8,128)(2,1)}, u32[]{:S(2)}) copy-start(bf16[1024,544]{0,1:T(8,128)(2,1)} %get-tuple-element.15) | copy-start | bytes 3342340
  75.6 3.9 %copy-start.16 = (bf16[11,128,1024]{2,1,0:T(8,128)(2,1)S(1)}, bf16[11,128,1024]{2,1,0:T(8,128)(2,1)}, u32[]{:S(2)}) copy-start(bf16[11,128,1024]{2,1,0:T(8,128)(2,1)} %all-gather.2.cloned.1.call-done) | copy-start | bytes 8650756
  83.1 4.8 %copy-start.7 = (f32[64,32,1,1]{0,1,3,2:T(8,128)S(1)}, f32[64,32,1,1]{0,1,3,2:T(8,128)}, u32[]{:S(2)}) copy-start(f32[64,32,1,1]{0,1,3,2:T(8,128)} %constant.70) | copy-start | bytes 24580
  87.9 5.2 %copy-start.1 = (f32[1408,544]{1,0:T(8,128)S(1)}, f32[1408,544]{1,0:T(8,128)}, u32[]{:S(2)}) copy-start(f32[1408,544]{1,0:T(8,128)} %copy.51) | copy-start | bytes 9191428
  98.1 7.8 %copy-start.2 = (f32[11,2,32,544]{3,2,1,0:T(8,128)S(1)}, f32[11,2,32,544]{3,2,1,0:T(8,128)}, u32[]{:S(2)}) copy-start(f32[11,2,32,544]{3,2,1,0:T(8,128)} %get-tuple-element.30) | copy-start | bytes 4595716
  111.1 1.3 copy-start.19
  111.1 52.6 %copy-start.9 = (f32[544]{0:T(1024)S(1)}, f32[544]{0:T(1024)}, u32[]{:S(2)}) copy-start(f32[544]{0:T(1024)} %constant.60.clone) | copy-start | bytes 6532
  161.0 3.6 %copy-start = (f32[1024,544]{0,1:T(8,128)S(1)}, f32[1024,544]{0,1:T(8,128)}, u32[]{:S(2)}) copy-start(f32[1024,544]{0,1:T(8,128)} %sub.49) | copy-start | bytes 6684676
  165.7 3.6 %collective-permute-start = (f32[1,4,1]{1,2,0:T(1,128)S(1)}, f32[1,4,1]{1,2,0:T(1,128)S(1)}, u32[]{:S(2)}, u32[]{:S(2)}) collective-permute-start(f32[1,4,1]{1,2,0:T(1,128)S(1)} %bitcast.113), channel_id=1, source_target_pairs={{0,1},{1,0},{2,3},{3,2},{4,5},{5,4},{6,7},{7,6},{8,9},{9,8},{10,11... | collective-permute-start | bytes 56 | tf_op jit(solution)/shard_map/ppermute | solution.py:25
  169.3 1.2 collective-permute-start.1
  170.5 3.6 %collective-permute-start.2 = (f32[4,4,1]{1,2,0:T(1,128)S(1)}, f32[4,4,1]{1,2,0:T(1,128)S(1)}, u32[]{:S(2)}, u32[]{:S(2)}) collective-permute-start(f32[4,4,1]{1,2,0:T(1,128)S(1)} %pad_maximum_fusion.2), channel_id=1, source_target_pairs={{0,4},{1,5},{2,6},{3,7},{4,0},{5,1},{6,2},{7,3},{8,12},{9,13},{10,... | collective-permute-start | bytes 200 | tf_op jit(solution)/shard_map/ppermute | solution.py:25
  174.2 3.7 %collective-permute-start.3 = (f32[8,4,1]{1,2,0:T(1,128)S(1)}, f32[8,4,1]{1,2,0:T(1,128)S(1)}, u32[]{:S(2)}, u32[]{:S(2)}) collective-permute-start(f32[8,4,1]{1,2,0:T(1,128)S(1)} %pad_maximum_fusion.1), channel_id=1, source_target_pairs={{0,8},{1,9},{2,10},{3,11},{4,12},{5,13},{6,14},{7,15},{8,0},{9,1},... | collective-permute-start | bytes 392 | tf_op jit(solution)/shard_map/ppermute | solution.py:25
  178.1 4.5 %collective-permute-start.4 = (f32[16,4,1]{0,1,2:T(4,128)S(1)}, f32[16,4,1]{0,1,2:T(4,128)S(1)}, u32[]{:S(2)}, u32[]{:S(2)}) collective-permute-start(f32[16,4,1]{0,1,2:T(4,128)S(1)} %pad_maximum_fusion.3), channel_id=1, source_target_pairs={{0,16},{1,17},{2,18},{3,19},{4,20},{5,21},{6,22},{7,23},{8,24},{9,... | collective-permute-start | bytes 776 | tf_op jit(solution)/shard_map/ppermute | solution.py:25
Sparse Core Ops, SparseCore 0:
  10.2 47.0 all-gather.1
  112.4 48.5 all-reduce.2
